TPU v7x, 32 devices: a whole 2x2x4 slice. The times are simulated.
32 devices in a mesh: tile: 8 (over y, x, core), dir: 4 (over z).
Axes of the slice: x: 2, y: 2, z: 4, core: 2. Of those that a mesh axis runs over, the one named last changes fastest.
Arguments:
- screens: bfloat16 [6, 512, 2048], P(None, 'tile'), may hold values from -13 to 13
- ray_shift: int32 [16, 6, 2], P('dir'), may hold values from -128 to 2047, as said below
- ray_weight: float32 [16, 6, 4], P('dir'), may hold values from 0 to 0.5
- influence_index: int32 [512, 16, 16], P('tile', 'dir'), may hold values from 0 to 69, as said below
- influence: bfloat16 [512, 16, 16, 128], P('tile', 'dir'), may hold values from 0 to 0.22
- pupil_mask: int32 [512, 2048], P('tile', 'dir'), may hold values 0 or 1
- petal: int32 [24, 48], P('tile', 'dir'), may hold values from 0 to 6
Outputs:
- commands: float32 [24, 48], P('tile', 'dir')
- corrected: bfloat16 [16, 512, 2048], P('dir', 'tile')
Inputs may be any that keep to these rules, and one draw needn't show every extreme that they name: ray_shift[..., 0], the row offset, lies in -128 to 127 and reaches both ends; ray_shift[..., 1], the column offset, lies in 0 to 2047. `influence_index`: each entry names a grid point of the tile's own actuator block extended by one actuator on each side, flattened row by row with 14 points a row; entries may repeat.
All inputs are finite; a program needn't handle non-finite values. No bound on the sum of `pupil_mask` on one device may be relied on, other than what follows from the above.
Results may differ from a plain program's by a relative error of at most 0.007.
Values may be sent and summed in bfloat16 or wider, within the bound.
No kernel may reach another device: no remote copies, remote signals or barrier semaphores. Data moves between devices by JAX's collectives and lax.ppermute only.
A program may use at most 128 MiB of HBM per device.

v0:
```python
import jax
import jax.numpy as jnp
from jax import lax
from jax.sharding import PartitionSpec as P

SPAN = 2
AR_DEV = 3
AC_DEV = 12
ITERS = 3
ridge_weight = 1.0
piston_weight = 0.002
highest = lax.Precision.HIGHEST


def passed_along(array, axis, by):
    size = lax.axis_size(axis)
    return lax.ppermute(array, axis, [(i, (i + by) % size) for i in range(size)])


def padded_2(array, sides, width):
    for axis, dim in sides:
        size, length = (lax.axis_size(axis), array.shape[dim])
        up = [(i, (i + 1) % size) for i in range(size - 1)]
        down = [(j, i) for i, j in up]
        last = lax.slice_in_dim(array, length - width, length, axis=dim)
        first = lax.slice_in_dim(array, 0, width, axis=dim)
        before = lax.ppermute(last, axis, up)
        after = lax.ppermute(first, axis, down)
        array = jnp.concatenate([before, array, after], axis=dim)
    return array


def band_stack_whole(piece):
    bands = []
    for offset in range(SPAN, -SPAN - 1, -1):
        if offset == 0:
            bands.append(piece)
        else:
            bands.append(passed_along(piece, "tile", offset))
    return jnp.concatenate(bands, axis=1)


def trace_rows(padded_rim, shifts, layer_gains, rim_depth, band_rows):
    summed = jnp.zeros((band_rows, padded_rim.shape[2]), jnp.float32)
    for layer_index in range(padded_rim.shape[0]):
        window = lax.dynamic_slice_in_dim(
            padded_rim[layer_index], rim_depth + shifts[layer_index, 0], band_rows + 1, 0
        ).astype(jnp.float32)
        window = jnp.roll(window, -shifts[layer_index, 1], axis=1)
        beside = jnp.roll(window, -1, axis=1)
        gains = layer_gains[layer_index]
        summed = summed + (
            gains[0] * window[:-1]
            + gains[1] * beside[:-1]
            + gains[2] * window[1:]
            + gains[3] * beside[1:]
        )
    return summed


def fold_rims(gathered):
    padded = padded_2(gathered, (("tile", 0), ("dir", 1)), 1)
    grid_rows = gathered.shape[0] - 2
    grid_columns = gathered.shape[1] - 2
    interior = gathered[1:-1, 1:-1]
    interior = interior.at[:, 0].add(padded[2 : grid_rows + 2, 0])
    interior = interior.at[:, -1].add(padded[2 : grid_rows + 2, -1])
    interior = interior.at[0, :].add(padded[0, 2 : grid_columns + 2])
    interior = interior.at[-1, :].add(padded[-1, 2 : grid_columns + 2])
    interior = interior.at[0, 0].add(padded[0, 0])
    interior = interior.at[0, -1].add(padded[0, -1])
    interior = interior.at[-1, 0].add(padded[-1, 0])
    interior = interior.at[-1, -1].add(padded[-1, -1])
    return interior


def on_device(screens, ray_shift, ray_weight, influence_index, influence, pupil_mask, petal):
    band_rows = screens.shape[1]
    rim_depth = SPAN * band_rows
    padded_rim = band_stack_whole(screens)
    phases = [
        trace_rows(padded_rim, ray_shift[member], ray_weight[member], rim_depth, band_rows)
        for member in range(ray_shift.shape[0])
    ]
    direction_count = ray_shift.shape[0] * lax.axis_size("dir")
    summed = phases[0]
    for member in range(1, len(phases)):
        summed = summed + phases[member]
    mean_phase = (
        lax.psum_scatter(
            summed.astype(jnp.bfloat16), "dir", scatter_dimension=1, tiled=True
        ).astype(jnp.float32)
        / direction_count
    )
    tiles_here = influence.shape[1]
    near_count = influence.shape[2]
    values = influence.astype(jnp.float32)
    extent = (AR_DEV + 2) * (AC_DEV + 2)
    selector = (
        influence_index.reshape(-1)[:, None] == jnp.arange(extent, dtype=jnp.int32)[None, :]
    ).astype(jnp.float32)
    weights = pupil_mask.astype(jnp.float32)
    active = (petal < 6).astype(jnp.float32)
    petals = (petal.reshape(-1)[:, None] == jnp.arange(6, dtype=jnp.int32)[None, :]).astype(
        jnp.float32
    )

    def surface(commands):
        extended = padded_2(commands, (("tile", 0), ("dir", 1)), 1)
        picked = jnp.dot(selector, extended.reshape(-1), precision=highest).reshape(
            band_rows, tiles_here, near_count
        )
        tile_sums = jnp.einsum("rckp,rck->rcp", values, picked, precision=highest)
        return tile_sums.reshape(band_rows, tiles_here * 128)

    def spread(field):
        tile_terms = jnp.einsum(
            "rckp,rcp->rck", values, field.reshape(band_rows, tiles_here, 128), precision=highest
        )
        gathered = jnp.dot(tile_terms.reshape(-1), selector, precision=highest).reshape(
            AR_DEV + 2, AC_DEV + 2
        )
        return fold_rims(gathered)

    def global_norm(residual):
        return lax.psum(jnp.sum(residual * residual), ("tile", "dir"))

    rhs = active * spread(weights * mean_phase)
    commands = jnp.zeros_like(rhs)
    residual = rhs
    direction = rhs
    norm_now = global_norm(residual)
    for step_index in range(ITERS):
        local_part = active * spread(weights * surface(direction)) + ridge_weight * direction
        local_totals = jnp.dot(direction.reshape(-1), petals, precision=highest)
        petal_totals, partial_dot = lax.psum(
            (local_totals, jnp.sum(direction * local_part)), ("tile", "dir")
        )
        applied = local_part + piston_weight * jnp.dot(
            petals, petal_totals, precision=highest
        ).reshape(direction.shape)
        curvature = partial_dot + piston_weight * jnp.sum(petal_totals * petal_totals)
        step_size = norm_now / curvature
        commands = commands + step_size * direction
        residual = residual - step_size * applied
        norm_next = global_norm(residual)
        direction = residual + norm_next / norm_now * direction
        norm_now = norm_next
    fitted = surface(commands)
    whole_band = lax.all_gather(fitted.astype(jnp.bfloat16), "dir", axis=1, tiled=True).astype(
        fitted.dtype
    )
    corrected = jnp.stack([(phase_rows - whole_band).astype(jnp.bfloat16) for phase_rows in phases])
    return (commands, corrected)


def solution(mesh):
    in_specs = (
        P(None, "tile", None),
        P("dir", None, None),
        P("dir", None, None),
        P("tile", "dir", None),
        P("tile", "dir", None, None),
        P("tile", "dir"),
        P("tile", "dir"),
    )
    out_specs = (P("tile", "dir"), P("dir", "tile", None))
    return jax.shard_map(
        on_device, mesh=mesh, in_specs=in_specs, out_specs=out_specs, check_vma=False
    )
```

profile of v0, /device:TPU:4, one launch (start us, length us, event | category | flops | bytes accessed | tf_op | source)
XLA Modules:
  0.0 727.7 jit_solution(10193905271201965904)
XLA Ops:
  8.8 2.6 collective-permute-start.2
  70.6 6.6 collective-permute-done.1
  80.4 30.4 %collective-permute-done.3 = bf16[6,64,2048]{2,1,0:T(8,128)(2,1)S(1)} collective-permute-done((bf16[6,64,2048]{2,1,0:T(8,128)(2,1)}, bf16[6,64,2048]{2,1,0:T(8,128)(2,1)S(1)}, u32[]{:S(2)}, u32[]{:S(2)}) %collective-permute-start.3) | collective-permute-done | bytes 1572896 | tf_op jit(solution)/shard_map/ppermute | solution.py:17
  162.1 96.7 %add_convert_fusion = (bf16[64,2048]{1,0:T(8,128)(2,1)}, f32[64,2048]{1,0:T(8,128)}, f32[64,2048]{1,0:T(8,128)}, f32[64,2048]{1,0:T(8,128)}, f32[64,2048]{1,0:T(8,128)}) fusion(f32[65,1]{1,0:T(8,128)} %slice.2466, f32[65,2047]{1,0:T(8,128)} %slice.2465, f32[]{:T(128)} %bitcast.97, f32[65,2048]{1,0:T(8,128)} %copy-done.28, f32[]{:T(128)} %bitcast.96, ...), kind=kLoop, calls=%fused_computation.395 | loop fusion | flops 31457280 | bytes 40305024 | tf_op jit(solution)/shard_map/convert_element_type | solution.py:91
  262.5 17.6 %reduce-scatter.2.cloned.1.call-done = bf16[64,512]{1,0:T(8,128)(2,1)} async-done(((bf16[64,2048]{1,0:T(8,128)(2,1)}), bf16[64,512]{1,0:T(8,128)(2,1)}) %reduce-scatter.2.cloned.1.call-update) | async-done | bytes 65552 | tf_op jit(solution)/shard_map/reduce_scatter | solution.py:90
  284.2 1.9 collective-permute-start.4
  286.2 4.5 collective-permute-start.5
  295.5 3.4 collective-permute-done.7
  301.8 1.8 dynamic-slice.243
  312.1 1.9 collective-permute-start.8
  314.0 4.5 collective-permute-start.9
  319.9 3.7 collective-permute-start.10
  324.9 4.2 collective-permute-done.11
  329.3 2.5 fusion.21
  336.1 1.9 collective-permute-start.12
  338.0 4.5 collective-permute-start.13
  343.9 2.4 collective-permute-start.14
  348.4 3.4 collective-permute-done.15
  354.7 1.8 dynamic-slice.244
  365.5 38.8 %all-reduce.2 = (f32[6]{0:T(128)S(1)}, f32[]{:T(128)}, f32[]{:T(128)}) all-reduce(f32[6]{0:T(128)S(1)} %convolution_bitcast_fusion.4, f32[]{:T(128)} %get-tuple-element.388, f32[]{:T(128)} %get-tuple-element.387), channel_id=1, replica_groups=mesh['tile'=8,'dir'=4] {'tile','dir'}, use_global_device_ids=true, to_apply=%region_7.9 | all-reduce | flops 8 | bytes 64 | tf_op jit(solution)/shard_map/psum | solution.py:136
  407.9 42.2 %psum.66 = f32[]{:T(128)} all-reduce(f32[]{:T(128)} %get-tuple-element.398), channel_id=1, replica_groups=mesh['tile'=8,'dir'=4] {'tile','dir'}, use_global_device_ids=true, to_apply=%region_10.12 | all-reduce | flops 1 | bytes 8 | tf_op jit(solution)/shard_map/psum | solution.py:126
  451.6 1.9 collective-permute-start.16
  453.5 4.5 collective-permute-start.17
  459.4 1.9 collective-permute-start.18
  462.7 4.2 collective-permute-done.19
  467.0 2.5 fusion.19
  473.8 1.9 collective-permute-start.20
  475.7 4.5 collective-permute-start.21
  481.6 2.6 collective-permute-start.22
  486.3 3.4 collective-permute-done.23
  503.2 40.5 %all-reduce.1 = (f32[6]{0:T(128)S(1)}, f32[]{:T(128)}) all-reduce(f32[6]{0:T(128)S(1)} %convolution_bitcast_fusion.2, f32[]{:T(128)} %multiply_reduce_fusion.1), channel_id=1, replica_groups=mesh['tile'=8,'dir'=4] {'tile','dir'}, use_global_device_ids=true, to_apply=%region_13.15 | all-reduce | flops 7 | bytes 56 | tf_op jit(solution)/shard_map/psum | solution.py:136
  547.3 40.2 %psum.69 = f32[]{:T(128)} all-reduce(f32[]{:T(128)} %get-tuple-element.396), channel_id=1, replica_groups=mesh['tile'=8,'dir'=4] {'tile','dir'}, use_global_device_ids=true, to_apply=%region_16.18 | all-reduce | flops 1 | bytes 8 | tf_op jit(solution)/shard_map/psum | solution.py:126
  589.0 1.9 collective-permute-start.24
  591.0 4.5 collective-permute-start.25
  596.9 3.9 collective-permute-start.26
  602.3 3.9 collective-permute-done.27
  606.4 2.5 fusion.17
  613.2 1.9 collective-permute-start.28
  615.1 4.5 collective-permute-start.29
  621.0 2.6 collective-permute-start.30
  625.8 3.4 collective-permute-done.31
  642.7 38.8 %all-reduce = (f32[]{:T(128)}, f32[6]{0:T(128)S(1)}) all-reduce(f32[]{:T(128)} %fusion.224, f32[6]{0:T(128)S(1)} %convolution_bitcast_fusion), channel_id=1, replica_groups=mesh['tile'=8,'dir'=4] {'tile','dir'}, use_global_device_ids=true, to_apply=%region_18.20 | all-reduce | flops 7 | bytes 56 | tf_op jit(solution)/shard_map/psum | solution.py:136
  684.1 1.9 collective-permute-start.32
  686.1 4.5 collective-permute-start.33
  692.0 3.6 collective-permute-start.34
  696.9 4.2 collective-permute-done.35
  701.2 2.5 fusion.15
  705.0 14.3 %all_gather.3 = bf16[64,2048]{1,0:T(8,128)(2,1)S(1)} all-gather(bf16[64,512]{1,0:T(8,128)(2,1)S(1)} %bitcast.390), channel_id=1, replica_groups=mesh['tile'=8,'dir'=4] {'dir'}, dimensions={1}, use_global_device_ids=true | all-gather | bytes 327680 | tf_op jit(solution)/shard_map/all_gather | solution.py:150
  (392 shorter events, 146.2 us)
Async XLA Ops:
  7.2 274.0 %copy-start = (bf16[64,4,16,128]{3,2,1,0:T(8,128)(2,1)S(1)}, bf16[64,4,16,128]{3,2,1,0:T(8,128)(2,1)}, u32[]{:S(2)}) copy-start(bf16[64,4,16,128]{3,2,1,0:T(8,128)(2,1)} %param.77) | copy-start | bytes 3145732
  7.2 58.3 %copy-start.36 = (f32[4,6,4]{1,2,0:T(4,128)S(1)}, f32[4,6,4]{1,2,0:T(4,128)}, u32[]{:S(2)}) copy-start(f32[4,6,4]{1,2,0:T(4,128)} %param.75) | copy-start | bytes 1156
  7.2 56.9 %copy-start.39 = (s32[3,12]{1,0:T(4,128)S(1)}, s32[3,12]{1,0:T(4,128)}, u32[]{:S(2)}) copy-start(s32[3,12]{1,0:T(4,128)} %param.79) | copy-start | bytes 436
  7.2 272.9 %reduce-scatter.2.cloned.1.call-start = ((), (), s32[]{:S(2)}) async-start(), calls=%async_computation.1 | async-start | bytes 327680 | tf_op jit(solution)/shard_map/reduce_scatter | solution.py:90
  7.2 61.8 %collective-permute-start = (bf16[6,64,2048]{2,1,0:T(8,128)(2,1)}, bf16[6,64,2048]{2,1,0:T(8,128)(2,1)}, u32[]{:S(2)}, u32[]{:S(2)}) collective-permute-start(bf16[6,64,2048]{2,1,0:T(8,128)(2,1)} %param.73), channel_id=1, source_target_pairs={{0,8},{4,12},{8,16},{12,20},{16,24},{20,28},{24,0},{28,4},{1,9},{5... | collective-permute-start | bytes 4718600 | tf_op jit(solution)/shard_map/ppermute | solution.py:17
  8.8 68.4 %collective-permute-start.1 = (bf16[6,64,2048]{2,1,0:T(8,128)(2,1)}, bf16[6,64,2048]{2,1,0:T(8,128)(2,1)}, u32[]{:S(2)}, u32[]{:S(2)}) collective-permute-start(bf16[6,64,2048]{2,1,0:T(8,128)(2,1)} %param.73), channel_id=1, source_target_pairs={{0,4},{4,8},{8,12},{12,16},{16,20},{20,24},{24,28},{28,0},{1,5},{5... | collective-permute-start | bytes 4718600 | tf_op jit(solution)/shard_map/ppermute | solution.py:17
  8.8 70.1 %collective-permute-start.2 = (bf16[6,64,2048]{2,1,0:T(8,128)(2,1)}, bf16[6,64,2048]{2,1,0:T(8,128)(2,1)}, u32[]{:S(2)}, u32[]{:S(2)}) collective-permute-start(bf16[6,64,2048]{2,1,0:T(8,128)(2,1)} %param.73), channel_id=1, source_target_pairs={{0,28},{4,0},{8,4},{12,8},{16,12},{20,16},{24,20},{28,24},{1,29},{... | collective-permute-start | bytes 4718600 | tf_op jit(solution)/shard_map/ppermute | solution.py:17
  11.4 99.4 %collective-permute-start.3 = (bf16[6,64,2048]{2,1,0:T(8,128)(2,1)}, bf16[6,64,2048]{2,1,0:T(8,128)(2,1)S(1)}, u32[]{:S(2)}, u32[]{:S(2)}) collective-permute-start(bf16[6,64,2048]{2,1,0:T(8,128)(2,1)} %param.73), channel_id=1, source_target_pairs={{0,24},{4,28},{8,0},{12,4},{16,8},{20,12},{24,16},{28,20},{1,25},{... | collective-permute-start | bytes 4718600 | tf_op jit(solution)/shard_map/ppermute | solution.py:17
  260.8 22.3 %copy-start.38 = (s32[4096]{0:T(1024)S(1)}, s32[4096]{0:T(1024)}, u32[]{:S(2)}) copy-start(s32[4096]{0:T(1024)} %eq.69) | copy-start | bytes 49156
  281.1 30.9 %copy-start.40 = (s32[3,12]{1,0:T(4,128)S(1)}, s32[3,12]{1,0:T(4,128)}, u32[]{:S(2)}) copy-start(s32[3,12]{1,0:T(4,128)} %param.79) | copy-start | bytes 436
  281.1 37.4 %copy-start.41 = (s32[36]{0:T(128)S(1)}, s32[36]{0:T(128)}, u32[]{:S(2)}) copy-start(s32[36]{0:T(128)} %eq.77) | copy-start | bytes 436
  284.2 6.6 collective-permute-start.4
  286.2 5.8 collective-permute-start.5
  292.1 2.6 collective-permute-start.6
  293.4 5.5 collective-permute-start.7
  312.1 6.7 collective-permute-start.8
  314.0 5.8 collective-permute-start.9
  319.9 5.0 collective-permute-start.10
  323.6 5.5 collective-permute-start.11
  336.1 6.6 collective-permute-start.12
  338.0 5.8 collective-permute-start.13
  343.9 3.7 collective-permute-start.14
  346.3 5.5 collective-permute-start.15
  451.6 6.7 collective-permute-start.16
  453.5 5.8 collective-permute-start.17
  459.4 3.2 collective-permute-start.18
  461.4 5.5 collective-permute-start.19
  473.8 6.6 collective-permute-start.20
  475.7 5.8 collective-permute-start.21
  481.6 3.9 collective-permute-start.22
  484.2 5.5 collective-permute-start.23
  589.0 6.7 collective-permute-start.24
  591.0 5.8 collective-permute-start.25
  596.9 5.5 collective-permute-start.26
  600.8 5.5 collective-permute-start.27
  613.2 6.6 collective-permute-start.28
  615.1 5.8 collective-permute-start.29
  621.0 3.9 collective-permute-start.30
  623.7 5.5 collective-permute-start.31
  684.1 20.8 %copy-start.37 = (f32[3,12]{1,0:T(4,128)}, f32[3,12]{1,0:T(4,128)S(1)}, u32[]{:S(2)}) copy-start(f32[3,12]{1,0:T(4,128)S(1)} %multiply_add_fusion) | copy-start | bytes 436
  684.1 6.5 collective-permute-start.32
  686.1 5.8 collective-permute-start.33
  692.0 4.9 collective-permute-start.34
  695.6 5.5 collective-permute-start.35
  703.8 15.5 %copy-start.29 = (f32[64,2048]{1,0:T(8,128)S(1)}, f32[64,2048]{1,0:T(8,128)}, u32[]{:S(2)}) copy-start(f32[64,2048]{1,0:T(8,128)} %get-tuple-element.403) | copy-start | bytes 1572868
  703.8 15.5 %copy-start.30 = (f32[64,2048]{1,0:T(8,128)S(1)}, f32[64,2048]{1,0:T(8,128)}, u32[]{:S(2)}) copy-start(f32[64,2048]{1,0:T(8,128)} %get-tuple-element.404) | copy-start | bytes 1572868
  703.8 15.5 %copy-start.31 = (f32[64,2048]{1,0:T(8,128)S(1)}, f32[64,2048]{1,0:T(8,128)}, u32[]{:S(2)}) copy-start(f32[64,2048]{1,0:T(8,128)} %get-tuple-element.405) | copy-start | bytes 1572868
  703.8 15.5 %copy-start.32 = (f32[64,2048]{1,0:T(8,128)S(1)}, f32[64,2048]{1,0:T(8,128)}, u32[]{:S(2)}) copy-start(f32[64,2048]{1,0:T(8,128)} %get-tuple-element.406) | copy-start | bytes 1572868
  (35 other events, 104.8 us)
Sparse Core Ops, SparseCore 0:
  259.0 21.1 reduce-scatter.1
where the time goes:
time: 734 us; the launch traced here: 728 us
  blocking collectives  215 us (29%)
  other arithmetic  123 us (17%)
  between operations  96.2 us (13%)
  waiting for transfers between devices  94.2 us (13%)
  starting transfers between devices  89 us (12%)
  local copies, waits for them, and re-layouts  84.2 us (11%)
  matrix products  25.9 us (4%)
    psum x3, blocking collectives, on_device(): lax.psum((local_totals, jnp.sum(direction * local_part)), ('tile', 'dir'))  118 us
    convert_element_type x1, other arithmetic, on_device(): summed.astype(jnp.bfloat16)  96.7 us
    psum x2, blocking collectives, global_norm(): return lax.psum(jnp.sum(residual * residual), ('tile', 'dir'))  82.5 us
    ppermute x16, starting transfers between devices, padded_2(): after = lax.ppermute(first, axis, down)  46.9 us
    ppermute x16, waiting for transfers between devices, padded_2(): after = lax.ppermute(first, axis, down)  39.4 us
    slice x52, local copies, waits for them, and re-layouts, trace_rows(): beside = jnp.roll(window, -1, axis=1)  37.7 us
    ppermute x16, starting transfers between devices, padded_2(): before = lax.ppermute(last, axis, up)  37.3 us
    ppermute x4, waiting for transfers between devices, passed_along(): lax.ppermute(array, axis, [(i, (i + by) % size) for i in range(size)])  37 us
  transfers between devices with their start and end apart: 37, of which 19 were waited for; matrix products, arithmetic and copies ran while one was open for 3% of the time, Pallas kernels for 0%

commit v1 on v0

--- a/solution.py
+++ b/solution.py
@@ -134,7 +134,7 @@
         local_part = active * spread(weights * surface(direction)) + ridge_weight * direction
         local_totals = jnp.dot(direction.reshape(-1), petals, precision=highest)
         petal_totals, partial_dot = lax.psum(
-            (local_totals, jnp.sum(direction * local_part)), ("tile", "dir")
+            lax.psum((local_totals, jnp.sum(direction * local_part)), "dir"), "tile"
         )
         applied = local_part + piston_weight * jnp.dot(
             petals, petal_totals, precision=highest

time: 734 us -> 718 us (0.978)
  blocking collectives: 215 us -> 201 us
    psum x3 -> x6, blocking collectives: 118 us -> 66.1 us  [the longest x3 37.3 us: on_device(): lax.psum(lax.psum((local_totals, jnp.sum(direction * local_part)), 'dir')...]
    psum x2 -> x3, blocking collectives: 82.5 us -> 121 us  [global_norm(): return lax.psum(jnp.sum(residual * residual), ('tile', 'dir'))]
where the time goes in v1:
time: 718 us; the launch traced here: 711 us
  blocking collectives  201 us (28%)
  other arithmetic  122 us (17%)
  between operations  96.4 us (13%)
  waiting for transfers between devices  94.2 us (13%)
  starting transfers between devices  88.4 us (12%)
  local copies, waits for them, and re-layouts  83.6 us (12%)
  matrix products  25.9 us (4%)
    psum x3, blocking collectives, global_norm(): return lax.psum(jnp.sum(residual * residual), ('tile', 'dir'))  121 us
    convert_element_type x1, other arithmetic, on_device(): summed.astype(jnp.bfloat16)  96 us
    ppermute x16, starting transfers between devices, padded_2(): after = lax.ppermute(first, axis, down)  46.9 us
    ppermute x16, waiting for transfers between devices, padded_2(): after = lax.ppermute(first, axis, down)  39.9 us
    slice x52, local copies, waits for them, and re-layouts, trace_rows(): beside = jnp.roll(window, -1, axis=1)  37.6 us
    psum x3, blocking collectives, on_device(): lax.psum(lax.psum((local_totals, jnp.sum(direction * local_part)), 'dir')...  37.3 us
    ppermute x16, starting transfers between devices, padded_2(): before = lax.ppermute(last, axis, up)  36.7 us
    ppermute x4, waiting for transfers between devices, passed_along(): lax.ppermute(array, axis, [(i, (i + by) % size) for i in range(size)])  36.5 us
  transfers between devices with their start and end apart: 37, of which 19 were waited for; matrix products, arithmetic and copies ran while one was open for 3% of the time, Pallas kernels for 0%

profile of v1, /device:TPU:4, one launch (start us, length us, event | category | flops | bytes accessed | tf_op | source)
XLA Modules:
  0.0 711.0 jit_solution(13655085049809590970)
XLA Ops:
  8.8 2.6 collective-permute-start.2
  71.1 6.1 collective-permute-done.1
  80.4 30.4 %collective-permute-done.3 = bf16[6,64,2048]{2,1,0:T(8,128)(2,1)S(1)} collective-permute-done((bf16[6,64,2048]{2,1,0:T(8,128)(2,1)}, bf16[6,64,2048]{2,1,0:T(8,128)(2,1)S(1)}, u32[]{:S(2)}, u32[]{:S(2)}) %collective-permute-start.3) | collective-permute-done | bytes 1572896 | tf_op jit(solution)/shard_map/ppermute | solution.py:17
  162.0 96.0 %add_convert_fusion = (bf16[64,2048]{1,0:T(8,128)(2,1)}, f32[64,2048]{1,0:T(8,128)}, f32[64,2048]{1,0:T(8,128)}, f32[64,2048]{1,0:T(8,128)}, f32[64,2048]{1,0:T(8,128)}) fusion(f32[65,1]{1,0:T(8,128)} %slice.2466, f32[65,2047]{1,0:T(8,128)} %slice.2465, f32[]{:T(128)} %bitcast.97, f32[65,2048]{1,0:T(8,128)} %copy-done.28, f32[]{:T(128)} %bitcast.96, ...), kind=kLoop, calls=%fused_computation.395 | loop fusion | flops 31457280 | bytes 40305024 | tf_op jit(solution)/shard_map/convert_element_type | solution.py:91
  261.6 17.6 %reduce-scatter.2.cloned.1.call-done = bf16[64,512]{1,0:T(8,128)(2,1)} async-done(((bf16[64,2048]{1,0:T(8,128)(2,1)}), bf16[64,512]{1,0:T(8,128)(2,1)}) %reduce-scatter.2.cloned.1.call-update) | async-done | bytes 65552 | tf_op jit(solution)/shard_map/reduce_scatter | solution.py:90
  283.3 1.9 collective-permute-start.4
  285.3 4.5 collective-permute-start.5
  294.4 3.5 collective-permute-done.7
  311.0 1.9 collective-permute-start.8
  312.9 4.5 collective-permute-start.9
  318.8 3.7 collective-permute-start.10
  323.8 4.2 collective-permute-done.11
  328.2 2.5 fusion.21
  334.9 1.9 collective-permute-start.12
  336.9 4.5 collective-permute-start.13
  342.8 2.4 collective-permute-start.14
  347.2 3.5 collective-permute-done.15
  364.2 9.0 %all-reduce.5 = (f32[6]{0:T(128)S(1)}, f32[]{:T(128)}) all-reduce(f32[6]{0:T(128)S(1)} %convolution_bitcast_fusion.4, f32[]{:T(128)} %get-tuple-element.387), channel_id=1, replica_groups=mesh['tile'=8,'dir'=4] {'dir'}, use_global_device_ids=true, to_apply=%region_8.10 | all-reduce | flops 7 | bytes 56 | tf_op jit(solution)/shard_map/psum | solution.py:137
  373.2 12.4 %all-reduce.2 = (f32[6]{0:T(128)S(1)}, f32[]{:T(128)}) all-reduce(f32[6]{0:T(128)S(1)} %get-tuple-element.399, f32[]{:T(128)} %get-tuple-element.400), channel_id=1, replica_groups=mesh['tile'=8,'dir'=4] {'tile'}, use_global_device_ids=true, to_apply=%region_9.11 | all-reduce | flops 7 | bytes 56 | tf_op jit(solution)/shard_map/psum | solution.py:136
  386.4 40.6 %psum.105 = f32[]{:T(128)} all-reduce(f32[]{:T(128)} %get-tuple-element.388), channel_id=1, replica_groups=mesh['tile'=8,'dir'=4] {'tile','dir'}, use_global_device_ids=true, to_apply=%region_4.6 | all-reduce | flops 1 | bytes 8 | tf_op jit(solution)/shard_map/psum | solution.py:126
  429.7 40.4 %psum.110 = f32[]{:T(128)} all-reduce(f32[]{:T(128)} %get-tuple-element.403), channel_id=1, replica_groups=mesh['tile'=8,'dir'=4] {'tile','dir'}, use_global_device_ids=true, to_apply=%region_12.14 | all-reduce | flops 1 | bytes 8 | tf_op jit(solution)/shard_map/psum | solution.py:126
  473.5 4.5 collective-permute-start.17
  479.4 3.9 collective-permute-start.18
  484.6 4.2 collective-permute-done.19
  489.0 2.5 fusion.19
  495.7 1.9 collective-permute-start.20
  497.7 4.5 collective-permute-start.21
  503.6 2.5 collective-permute-start.22
  508.0 3.5 collective-permute-done.23
  524.9 9.5 %all-reduce.4 = (f32[6]{0:T(128)S(1)}, f32[]{:T(128)}) all-reduce(f32[6]{0:T(128)S(1)} %convolution_bitcast_fusion.2, f32[]{:T(128)} %multiply_reduce_fusion.1), channel_id=1, replica_groups=mesh['tile'=8,'dir'=4] {'dir'}, use_global_device_ids=true, to_apply=%region_16.18 | all-reduce | flops 7 | bytes 56 | tf_op jit(solution)/shard_map/psum | solution.py:137
  534.5 12.4 %all-reduce.1 = (f32[6]{0:T(128)S(1)}, f32[]{:T(128)}) all-reduce(f32[6]{0:T(128)S(1)} %get-tuple-element.397, f32[]{:T(128)} %get-tuple-element.398), channel_id=1, replica_groups=mesh['tile'=8,'dir'=4] {'tile'}, use_global_device_ids=true, to_apply=%region_17.19 | all-reduce | flops 7 | bytes 56 | tf_op jit(solution)/shard_map/psum | solution.py:136
  550.4 39.8 %psum.115 = f32[]{:T(128)} all-reduce(f32[]{:T(128)} %get-tuple-element.401), channel_id=1, replica_groups=mesh['tile'=8,'dir'=4] {'tile','dir'}, use_global_device_ids=true, to_apply=%region_20.22 | all-reduce | flops 1 | bytes 8 | tf_op jit(solution)/shard_map/psum | solution.py:126
  593.6 4.5 collective-permute-start.25
  599.6 2.5 collective-permute-start.26
  603.6 3.9 collective-permute-done.27
  607.7 2.5 fusion.17
  614.4 1.9 collective-permute-start.28
  616.4 4.5 collective-permute-start.29
  622.3 2.6 collective-permute-start.30
  626.9 3.5 collective-permute-done.31
  643.8 10.3 %all-reduce.3 = (f32[]{:T(128)}, f32[6]{0:T(128)S(1)}) all-reduce(f32[]{:T(128)} %fusion.224, f32[6]{0:T(128)S(1)} %convolution_bitcast_fusion), channel_id=1, replica_groups=mesh['tile'=8,'dir'=4] {'dir'}, use_global_device_ids=true, to_apply=%region_22.24 | all-reduce | flops 7 | bytes 56 | tf_op jit(solution)/shard_map/psum | solution.py:137
  654.1 12.4 %all-reduce = (f32[]{:T(128)}, f32[6]{0:T(128)S(1)}) all-reduce(f32[]{:T(128)} %get-tuple-element.395, f32[6]{0:T(128)S(1)} %get-tuple-element.396), channel_id=1, replica_groups=mesh['tile'=8,'dir'=4] {'tile'}, use_global_device_ids=true, to_apply=%region_23.25 | all-reduce | flops 7 | bytes 56 | tf_op jit(solution)/shard_map/psum | solution.py:136
  669.1 1.9 collective-permute-start.32
  671.0 4.5 collective-permute-start.33
  676.9 2.5 collective-permute-start.34
  680.7 4.2 collective-permute-done.35
  685.1 2.5 fusion.15
  688.8 13.8 %all_gather.3 = bf16[64,2048]{1,0:T(8,128)(2,1)S(1)} all-gather(bf16[64,512]{1,0:T(8,128)(2,1)S(1)} %bitcast.390), channel_id=1, replica_groups=mesh['tile'=8,'dir'=4] {'dir'}, dimensions={1}, use_global_device_ids=true | all-gather | bytes 327680 | tf_op jit(solution)/shard_map/all_gather | solution.py:150
  (396 shorter events, 152.4 us)
Async XLA Ops:
  7.2 273.1 %copy-start = (bf16[64,4,16,128]{3,2,1,0:T(8,128)(2,1)S(1)}, bf16[64,4,16,128]{3,2,1,0:T(8,128)(2,1)}, u32[]{:S(2)}) copy-start(bf16[64,4,16,128]{3,2,1,0:T(8,128)(2,1)} %param.77) | copy-start | bytes 3145732
  7.2 58.8 %copy-start.36 = (f32[4,6,4]{1,2,0:T(4,128)S(1)}, f32[4,6,4]{1,2,0:T(4,128)}, u32[]{:S(2)}) copy-start(f32[4,6,4]{1,2,0:T(4,128)} %param.75) | copy-start | bytes 1156
  7.2 57.5 %copy-start.39 = (s32[3,12]{1,0:T(4,128)S(1)}, s32[3,12]{1,0:T(4,128)}, u32[]{:S(2)}) copy-start(s32[3,12]{1,0:T(4,128)} %param.79) | copy-start | bytes 436
  7.2 272.0 %reduce-scatter.2.cloned.1.call-start = ((), (), s32[]{:S(2)}) async-start(), calls=%async_computation.1 | async-start | bytes 327680 | tf_op jit(solution)/shard_map/reduce_scatter | solution.py:90
  7.2 62.3 %collective-permute-start = (bf16[6,64,2048]{2,1,0:T(8,128)(2,1)}, bf16[6,64,2048]{2,1,0:T(8,128)(2,1)}, u32[]{:S(2)}, u32[]{:S(2)}) collective-permute-start(bf16[6,64,2048]{2,1,0:T(8,128)(2,1)} %param.73), channel_id=1, source_target_pairs={{0,8},{4,12},{8,16},{12,20},{16,24},{20,28},{24,0},{28,4},{1,9},{5... | collective-permute-start | bytes 4718600 | tf_op jit(solution)/shard_map/ppermute | solution.py:17
  8.8 68.4 %collective-permute-start.1 = (bf16[6,64,2048]{2,1,0:T(8,128)(2,1)}, bf16[6,64,2048]{2,1,0:T(8,128)(2,1)}, u32[]{:S(2)}, u32[]{:S(2)}) collective-permute-start(bf16[6,64,2048]{2,1,0:T(8,128)(2,1)} %param.73), channel_id=1, source_target_pairs={{0,4},{4,8},{8,12},{12,16},{16,20},{20,24},{24,28},{28,0},{1,5},{5... | collective-permute-start | bytes 4718600 | tf_op jit(solution)/shard_map/ppermute | solution.py:17
  8.8 70.1 %collective-permute-start.2 = (bf16[6,64,2048]{2,1,0:T(8,128)(2,1)}, bf16[6,64,2048]{2,1,0:T(8,128)(2,1)}, u32[]{:S(2)}, u32[]{:S(2)}) collective-permute-start(bf16[6,64,2048]{2,1,0:T(8,128)(2,1)} %param.73), channel_id=1, source_target_pairs={{0,28},{4,0},{8,4},{12,8},{16,12},{20,16},{24,20},{28,24},{1,29},{... | collective-permute-start | bytes 4718600 | tf_op jit(solution)/shard_map/ppermute | solution.py:17
  11.4 99.4 %collective-permute-start.3 = (bf16[6,64,2048]{2,1,0:T(8,128)(2,1)}, bf16[6,64,2048]{2,1,0:T(8,128)(2,1)S(1)}, u32[]{:S(2)}, u32[]{:S(2)}) collective-permute-start(bf16[6,64,2048]{2,1,0:T(8,128)(2,1)} %param.73), channel_id=1, source_target_pairs={{0,24},{4,28},{8,0},{12,4},{16,8},{20,12},{24,16},{28,20},{1,25},{... | collective-permute-start | bytes 4718600 | tf_op jit(solution)/shard_map/ppermute | solution.py:17
  259.9 22.3 %copy-start.38 = (s32[4096]{0:T(1024)S(1)}, s32[4096]{0:T(1024)}, u32[]{:S(2)}) copy-start(s32[4096]{0:T(1024)} %eq.69) | copy-start | bytes 49156
  280.2 30.7 %copy-start.40 = (s32[3,12]{1,0:T(4,128)S(1)}, s32[3,12]{1,0:T(4,128)}, u32[]{:S(2)}) copy-start(s32[3,12]{1,0:T(4,128)} %param.79) | copy-start | bytes 436
  280.2 37.2 %copy-start.41 = (s32[36]{0:T(128)S(1)}, s32[36]{0:T(128)}, u32[]{:S(2)}) copy-start(s32[36]{0:T(128)} %eq.77) | copy-start | bytes 436
  283.3 6.6 collective-permute-start.4
  285.3 5.8 collective-permute-start.5
  291.2 2.6 collective-permute-start.6
  292.5 5.5 collective-permute-start.7
  311.0 6.7 collective-permute-start.8
  312.9 5.8 collective-permute-start.9
  318.8 5.0 collective-permute-start.10
  322.5 5.5 collective-permute-start.11
  334.9 6.6 collective-permute-start.12
  336.9 5.8 collective-permute-start.13
  342.8 3.7 collective-permute-start.14
  345.2 5.5 collective-permute-start.15
  471.6 6.7 collective-permute-start.16
  473.5 5.8 collective-permute-start.17
  479.4 5.3 collective-permute-start.18
  483.3 5.5 collective-permute-start.19
  495.7 6.6 collective-permute-start.20
  497.7 5.8 collective-permute-start.21
  503.6 3.8 collective-permute-start.22
  506.1 5.5 collective-permute-start.23
  591.7 6.7 collective-permute-start.24
  593.6 5.8 collective-permute-start.25
  599.6 4.0 collective-permute-start.26
  602.0 5.5 collective-permute-start.27
  614.4 6.6 collective-permute-start.28
  616.4 5.8 collective-permute-start.29
  622.3 4.0 collective-permute-start.30
  624.9 5.5 collective-permute-start.31
  669.0 19.7 %copy-start.37 = (f32[3,12]{1,0:T(4,128)}, f32[3,12]{1,0:T(4,128)S(1)}, u32[]{:S(2)}) copy-start(f32[3,12]{1,0:T(4,128)S(1)} %multiply_add_fusion) | copy-start | bytes 436
  669.1 6.5 collective-permute-start.32
  671.0 5.8 collective-permute-start.33
  676.9 3.8 collective-permute-start.34
  679.4 5.5 collective-permute-start.35
  687.6 15.0 %copy-start.29 = (f32[64,2048]{1,0:T(8,128)S(1)}, f32[64,2048]{1,0:T(8,128)}, u32[]{:S(2)}) copy-start(f32[64,2048]{1,0:T(8,128)} %get-tuple-element.408) | copy-start | bytes 1572868
  687.6 15.0 %copy-start.30 = (f32[64,2048]{1,0:T(8,128)S(1)}, f32[64,2048]{1,0:T(8,128)}, u32[]{:S(2)}) copy-start(f32[64,2048]{1,0:T(8,128)} %get-tuple-element.409) | copy-start | bytes 1572868
  687.6 15.0 %copy-start.31 = (f32[64,2048]{1,0:T(8,128)S(1)}, f32[64,2048]{1,0:T(8,128)}, u32[]{:S(2)}) copy-start(f32[64,2048]{1,0:T(8,128)} %get-tuple-element.410) | copy-start | bytes 1572868
  687.6 15.0 %copy-start.32 = (f32[64,2048]{1,0:T(8,128)S(1)}, f32[64,2048]{1,0:T(8,128)}, u32[]{:S(2)}) copy-start(f32[64,2048]{1,0:T(8,128)} %get-tuple-element.411) | copy-start | bytes 1572868
  (35 other events, 104.0 us)
Sparse Core Ops, SparseCore 0:
  258.1 21.1 reduce-scatter.1
